TPU v7x, 32 devices: a whole 2x2x4 slice. The times are simulated.
32 devices in a mesh: seq: 8 (over z, x), dp: 4 (over y, core).
Axes of the slice: x: 2, y: 2, z: 4, core: 2. Of those that a mesh axis runs over, the one named last changes fastest.
Arguments:
- encoder_out: bfloat16 [4, 2560, 1536], P('dp', 'seq'), may hold values from -0.59765625 to 0.59765625
- out_grad: bfloat16 [4, 2560, 1536], P('dp', 'seq'), may hold values from -12 to 12
- segment_states: bfloat16 [4, 1024, 1536], P('dp', 'seq'), may hold values from -6 to 6
- segment_starts: int32 [4, 1024], P('dp', 'seq'), may hold values from 0 to 320, as said below
- segment_counts: int32 [4, 8], P('dp', 'seq'), may hold values from 32 to 128, as said below
- segment_probs: int32 [4, 1024], P('dp', 'seq'), may hold values from 0 to 65535, as said below
- query_weight: bfloat16 [1536, 1536], P('dp'), may hold values from -0.15625 to 0.15625
- key_weight: bfloat16 [1536, 1536], P('dp'), may hold values from -0.15625 to 0.15625
Outputs:
- x_grad: bfloat16 [4, 2560, 1536], P('dp', 'seq')
- segment_grad: bfloat16 [4, 1024, 1536], P('dp', 'seq')
Inputs may be any that keep to these rules, and one draw needn't show every extreme that they name: `segment_starts`: for block s of sequence b, the entries s * 128 + j with j < segment_counts[b, s] hold distinct increasing local positions below 320 at which segments start; the other entries hold 320. Byte 0 of every sequence starts a segment. `segment_counts`: every sequence has one block with exactly 128 segments and another with exactly a quarter of 128. `segment_probs`: A slot holds 0 exactly when it is past its block's count; slot 0 of every sequence holds 65535.
All inputs are finite; a program needn't handle non-finite values.
Results may differ from a plain program's by a relative error of at most 0.0049.
Values may be sent and summed in bfloat16 or wider, within the bound.
No kernel may reach another device: no remote copies, remote signals or barrier semaphores. Data moves between devices by JAX's collectives and lax.ppermute only.
A program may use at most 64 MiB of HBM per device.

v0:
```python
import jax
import jax.numpy as jnp
from jax import lax
from jax.sharding import PartitionSpec as P

prob_scale = 65536.0
norm_eps = 1e-06
exact = lax.Precision.HIGHEST
contract_last = (((1,), (1,)), ((), ()))
contract_first = (((0,), (0,)), ((), ()))


def shifted(block, axis, distance):
    devices = range(lax.axis_size(axis))
    route = [(i - distance, i) for i in devices if i - distance in devices]
    return lax.ppermute(block, axis, route)


def normalize_grad(vectors, scales, unit_grad):
    inner_prod = jnp.sum(vectors * unit_grad, axis=-1, keepdims=True)
    return scales * unit_grad - scales * scales * scales * inner_prod * vectors


def carry_from(log_keep, vectors, shard_index, from_lower):
    running_log = jnp.cumsum(log_keep)
    before = running_log - log_keep
    shard_order = jnp.arange(log_keep.shape[0])
    if from_lower:
        own_value = lax.dynamic_index_in_dim(before, shard_index, keepdims=False)
        selected = shard_order < shard_index
        log_gap = own_value - running_log
    else:
        own_value = lax.dynamic_index_in_dim(running_log, shard_index, keepdims=False)
        selected = shard_order > shard_index
        log_gap = before - own_value
    factor = jnp.where(selected, jnp.exp(jnp.where(selected, log_gap, 0.0)), 0.0)
    return jnp.dot(factor[None, :], vectors, precision=exact)


def per_device(
    encoder_out,
    out_grad,
    segment_states,
    segment_starts,
    segment_counts,
    segment_probs,
    query_weight,
    key_weight,
):
    token_rows = encoder_out[0]
    grad_rows = out_grad[0]
    token_count = token_rows.shape[0]
    slot_count = segment_states.shape[1]
    shard_index = lax.axis_index("seq")
    full_query, full_key = (
        lax.all_gather(query_weight, "dp", axis=0, tiled=True),
        lax.all_gather(key_weight, "dp", axis=0, tiled=True),
    )
    key_rows = jnp.dot(token_rows, full_key, preferred_element_type=jnp.float32)
    queries = jnp.dot(token_rows, full_query, preferred_element_type=jnp.float32)
    query_scale = lax.rsqrt(jnp.sum(queries * queries, axis=1, keepdims=True) + norm_eps)
    key_scale = lax.rsqrt(jnp.sum(key_rows * key_rows, axis=1, keepdims=True) + norm_eps)
    query_unit = queries * query_scale
    key_unit = key_rows * key_scale
    position = jnp.arange(token_count)
    later_rows = (shard_index > 0) | (position > 0)
    key_before = shifted(key_unit[token_count - 1 :], "seq", 1)
    key_prior = jnp.concatenate([key_before, key_unit[:-1]], axis=0)
    cosine = jnp.sum(query_unit * key_prior, axis=1)
    segment_total = segment_counts[0, 0]
    slot_index = jnp.arange(slot_count)
    slot_used = slot_index < segment_total
    start_pos = segment_starts[0]
    smoothing = jnp.where(slot_used, segment_probs[0].astype(jnp.float32) / prob_scale, 0.0)
    reached = slot_used[None, :] & (start_pos[None, :] <= position[:, None])
    member_id = jnp.sum(reached.astype(jnp.int32), axis=1) - 1
    membership = (member_id[:, None] == slot_index[None, :]).astype(jnp.float32)
    leading = (member_id < 0).astype(jnp.float32)
    starts = jnp.any(slot_used[None, :] & (start_pos[None, :] == position[:, None]), axis=1)
    running = jnp.cumsum(jnp.log(1.0 - smoothing))
    lower = slot_index[None, :] <= slot_index[:, None]
    decay_table = jnp.where(
        lower, jnp.exp(jnp.where(lower, running[:, None] - running[None, :], 0.0)), 0.0
    )
    weighted_states = smoothing[:, None] * segment_states[0].astype(jnp.float32)
    local_state = jnp.dot(decay_table, weighted_states, precision=exact)
    keep_all = jnp.exp(running)
    boundary_prob = jnp.where(later_rows, 0.5 * (1.0 - cosine), 1.0)
    confidence = jnp.where(starts, boundary_prob, 1.0 - boundary_prob)
    weighted_grad = confidence[:, None] * grad_rows
    slot_grad = lax.dot_general(membership, weighted_grad, contract_first, precision=exact)
    lead_grad = jnp.dot(leading[None, :], weighted_grad, precision=exact)
    back_vector = lead_grad + jnp.dot(keep_all[None, :], slot_grad, precision=exact)
    last_log = running[slot_count - 1 :]
    last_state = local_state[slot_count - 1 :]
    summaries = (
        lax.all_gather(last_log, "seq", axis=0, tiled=True),
        lax.all_gather(last_state, "seq", axis=0, tiled=True),
        lax.all_gather(last_log, "seq", axis=0, tiled=True),
        lax.all_gather(back_vector, "seq", axis=0, tiled=True),
    )
    state_in = carry_from(summaries[0], summaries[1], shard_index, True)
    grad_in = carry_from(summaries[2], summaries[3], shard_index, False)
    smoothed = local_state + keep_all[:, None] * state_in
    picked = jnp.dot(membership, smoothed, precision=exact) + leading[:, None] * state_in
    conf_grad = jnp.sum(grad_rows * picked, axis=1)
    cos_grad = jnp.where(later_rows, jnp.where(starts, -0.5 * conf_grad, 0.5 * conf_grad), 0.0)
    reach_end = jnp.exp(running[slot_count - 1] - running)
    state_grad = (
        lax.dot_general(decay_table, slot_grad, contract_first, precision=exact)
        + reach_end[:, None] * grad_in
    )
    segment_grad = (smoothing[:, None] * state_grad).astype(jnp.bfloat16)
    unit_q_grad = cos_grad[:, None] * key_prior
    prior_grad = cos_grad[:, None] * query_unit
    query_grad = normalize_grad(queries, query_scale, unit_q_grad).astype(jnp.bfloat16)
    from_next = shifted(prior_grad[:1], "seq", -1)
    unit_k_grad = jnp.concatenate([prior_grad[1:], from_next], axis=0)
    key_grad = normalize_grad(key_rows, key_scale, unit_k_grad).astype(jnp.bfloat16)
    x_grad = lax.dot_general(
        query_grad, full_query, contract_last, preferred_element_type=jnp.float32
    )
    x_grad = x_grad + lax.dot_general(
        key_grad, full_key, contract_last, preferred_element_type=jnp.float32
    )
    return (x_grad.astype(jnp.bfloat16)[None], segment_grad[None])


def solution(mesh):
    placed = (
        P("dp", "seq", None),
        P("dp", "seq", None),
        P("dp", "seq", None),
        P("dp", "seq"),
        P("dp", "seq"),
        P("dp", "seq"),
        P("dp", None),
        P("dp", None),
    )
    return jax.shard_map(
        per_device,
        mesh=mesh,
        in_specs=placed,
        out_specs=(P("dp", "seq", None), P("dp", "seq", None)),
        check_vma=False,
    )
```

profile of v0, /device:TPU:0, one launch (start us, length us, event | category | flops | bytes accessed | tf_op | source)
XLA Modules:
  0.0 151.8 jit_solution(7152754689850499982)
XLA Ops:
  7.3 0.7 all-gather.7.cloned.1.call-update
  8.0 0.7 all-gather.9.cloned.1.call-update
  10.8 1.3 bitcast_dynamic-update-slice_fusion
  12.1 23.1 %all-reduce = f32[8]{0:T(128)S(1)} all-reduce(f32[8]{0:T(128)S(1)} %bitcast_dynamic-update-slice_fusion), channel_id=2, replica_groups=mesh['seq'=8,'dp'=4] {'seq'}, use_global_device_ids=true, to_apply=%add | all-reduce | flops 8 | bytes 64
  36.1 0.9 fusion.24
  37.0 30.7 %all-gather.2 = f32[8,1,1536]{2,1,0:T(1,128)S(1)} all-gather(f32[1,1,1536]{2,1,0:T(1,128)S(1)} %slice_bitcast_fusion), channel_id=1, replica_groups=mesh['seq'=8,'dp'=4] {'seq'}, dimensions={0}, use_global_device_ids=true | all-gather | bytes 55296 | tf_op jit(solution)/shard_map/all_gather | solution.py:98
  67.7 0.8 convolution_reduce_fusion.2
  68.9 0.6 subtract_exponential_fusion
  69.6 1.5 fusion.8
  71.1 4.2 %multiply_reduce_fusion.4 = (f32[320]{0:T(512)S(1)}, f32[320,1536]{1,0:T(8,128)S(1)}) fusion(bf16[1536,1536]{1,0:T(8,128)(2,1)} %all-gather.7.cloned.1.call-done, bf16[1,320,1536]{2,1,0:T(8,128)(2,1)S(1)} %copy-done), kind=kOutput, calls=%fused_computation.20 | convolution fusion | flops 1510932224 | bytes 7668992 | tf_op jit(solution)/shard_map/dot_general | solution.py:60
  75.5 1.3 collective-permute-start.1
  76.8 1.4 slice.33
  78.3 10.6 %all-gather.9.cloned.1.call-done = bf16[1536,1536]{1,0:T(8,128)(2,1)} async-done(((bf16[384,1536]{1,0:T(8,128)(2,1)}), bf16[1536,1536]{1,0:T(8,128)(2,1)}) %all-gather.9.cloned.1.call-update) | async-done | bytes 4718608 | tf_op jit(solution)/shard_map/all_gather | solution.py:57
  88.9 4.8 %multiply_reduce_fusion.1 = (f32[320]{0:T(512)S(1)}, f32[320]{0:T(512)S(1)}, f32[320,1536]{1,0:T(8,128)S(1)}) fusion(f32[1,1536]{1,0:T(1,128)S(1)} %collective-permute-done.1, f32[319,1536]{1,0:T(8,128)} %slice.33, bf16[1536,1536]{1,0:T(8,128)(2,1)} %all-gather.9.cloned.1.call-done, bf16[1,320,1536]{2,1,0:T(8,128)(2,1)S(1)} %copy-done), kind=kOutput, calls=%fused_computation.16 | convolution fusion | flops 1512406528 | bytes 9636352 | tf_op jit(solution)/shard_map/dot_general | solution.py:59
  93.9 3.4 %collective-permute-start = (f32[1,1536]{1,0:T(1,128)S(1)}, f32[1,1536]{1,0:T(1,128)S(1)}, u32[]{:S(2)}, u32[]{:S(2)}) collective-permute-start(f32[1,1536]{1,0:T(1,128)S(1)} %slice.31), channel_id=1, source_target_pairs={{0,4},{4,8},{8,12},{12,16},{16,20},{20,24},{24,28},{1,5},{5,9},{9,... | collective-permute-start | bytes 18440 | tf_op jit(solution)/shard_map/ppermute | solution.py:16
  97.9 0.7 collective-permute-done
  98.7 0.8 multiply_reduce_fusion
  99.9 1.2 fusion.7
  101.1 0.9 fusion.9
  102.6 32.6 %all-gather.3 = f32[8,1,1536]{2,1,0:T(1,128)S(1)} all-gather(f32[1,1,1536]{2,1,0:T(1,128)S(1)} %reshape.174), channel_id=3, replica_groups=mesh['seq'=8,'dp'=4] {'seq'}, dimensions={0}, use_global_device_ids=true | all-gather | bytes 55296 | tf_op jit(solution)/shard_map/all_gather | solution.py:100
  135.2 0.8 convolution_reduce_fusion.1
  136.0 1.7 %fusion.5 = bf16[1,128,1536]{2,1,0:T(8,128)(2,1)} fusion(f32[128,1536]{1,0:T(8,128)S(1)} %fusion.7, f32[1536]{0:T(1024)S(1)} %convolution_reduce_fusion.1, f32[128]{0:T(128)S(1)} %get-tuple-element.10, f32[128]{0:T(128)S(1)} %bitcast_select_fusion, f32[128]{0:T(128)S(1)} %reduce), kind=kOutput, calls=%fused_computation.9 | convolution fusion | flops 302841856 | bytes 1187328 | tf_op jit(solution)/shard_map/dot_general | solution.py:110
  137.7 4.3 %fusion.10 = f32[320,1536]{1,0:T(8,128)S(1)} fusion(bf16[1536,1536]{1,0:T(8,128)(2,1)} %all-gather.7.cloned.1.call-done, f32[320,1536]{1,0:T(8,128)S(1)} %get-tuple-element.13, f32[319,1536]{1,0:T(8,128)S(1)} %bitcast.85, f32[1,1536]{1,0:T(1,128)S(1)} %collective-permute-done, f32[320]{0:T(512)S(1)} %get-tuple-element.16, f32[320]{0:T(512)S(1)} %select_select_fusion, ...), kind=kOutput, calls=%fused_computation.27 | convolution fusion | flops 1512898560 | bytes 10620672 | tf_op jit(solution)/shard_map/dot_general | solution.py:120
  142.1 2.9 %fusion.2 = bf16[1,320,1536]{2,1,0:T(8,128)(2,1)} fusion(f32[320,1536]{1,0:T(8,128)S(1)} %fusion.10, bf16[1536,1536]{1,0:T(8,128)(2,1)S(1)} %bitcast.89, f32[320,1536]{1,0:T(8,128)S(1)} %get-tuple-element.14, f32[1,1536]{1,0:T(1,128)S(1)} %collective-permute-done.1, f32[319,1536]{1,0:T(8,128)S(1)} %copy-done.3, f32[320]{0:T(512)S(1)} %get-tuple-element.8, ...), kind=kOutput, calls=%fused_computation.4 | convolution fusion | flops 1513390080 | bytes 11602432 | tf_op jit(solution)/shard_map/dot_general | solution.py:123
  (55 shorter events, 4.8 us)
Async XLA Ops:
  7.2 63.9 %copy-start = (bf16[1,320,1536]{2,1,0:T(8,128)(2,1)S(1)}, bf16[1,320,1536]{2,1,0:T(8,128)(2,1)}, u32[]{:S(2)}) copy-start(bf16[1,320,1536]{2,1,0:T(8,128)(2,1)} %param.8) | copy-start | bytes 2949124
  7.2 3.1 %copy-start.7 = (u32[32]{0:T(128)S(1)}, u32[32]{0:T(128)}, u32[]{:S(2)}) copy-start(u32[32]{0:T(128)} %constant.53) | copy-start | bytes 388
  7.2 2.2 %copy-start.6 = (s32[1,128]{1,0:T(1,128)S(1)}, s32[1,128]{1,0:T(1,128)}, u32[]{:S(2)}) copy-start(s32[1,128]{1,0:T(1,128)} %param.13) | copy-start | bytes 1540
  7.2 28.9 %copy-start.4 = (bf16[1,128,1536]{2,1,0:T(8,128)(2,1)S(1)}, bf16[1,128,1536]{2,1,0:T(8,128)(2,1)}, u32[]{:S(2)}) copy-start(bf16[1,128,1536]{2,1,0:T(8,128)(2,1)} %param.10) | copy-start | bytes 1179652
  7.2 61.4 %copy-start.5 = (s32[1,128]{1,0:T(1,128)S(1)}, s32[1,128]{1,0:T(1,128)}, u32[]{:S(2)}) copy-start(s32[1,128]{1,0:T(1,128)} %param.11) | copy-start | bytes 1540
  7.2 62.3 %copy-start.1 = (bf16[1,320,1536]{2,1,0:T(8,128)(2,1)S(1)}, bf16[1,320,1536]{2,1,0:T(8,128)(2,1)}, u32[]{:S(2)}) copy-start(bf16[1,320,1536]{2,1,0:T(8,128)(2,1)} %param.9) | copy-start | bytes 2949124
  7.2 63.8 %all-gather.7.cloned.1.call-start = ((), (), s32[]{:S(2)}) async-start(), calls=%async_computation | async-start | bytes 5898240 | tf_op jit(solution)/shard_map/all_gather | solution.py:56
  8.0 80.9 %all-gather.9.cloned.1.call-start = ((), (), s32[]{:S(2)}) async-start(), calls=%async_computation.1 | async-start | bytes 5898240 | tf_op jit(solution)/shard_map/all_gather | solution.py:57
  75.5 13.4 %collective-permute-start.1 = (f32[1,1536]{1,0:T(1,128)S(1)}, f32[1,1536]{1,0:T(1,128)S(1)}, u32[]{:S(2)}, u32[]{:S(2)}) collective-permute-start(f32[1,1536]{1,0:T(1,128)S(1)} %slice.34), channel_id=1, source_target_pairs={{4,0},{8,4},{12,8},{16,12},{20,16},{24,20},{28,24},{5,1},{9,5},{13... | collective-permute-start | bytes 18440 | tf_op jit(solution)/shard_map/ppermute | solution.py:16
  93.9 4.7 %collective-permute-start = (f32[1,1536]{1,0:T(1,128)S(1)}, f32[1,1536]{1,0:T(1,128)S(1)}, u32[]{:S(2)}, u32[]{:S(2)}) collective-permute-start(f32[1,1536]{1,0:T(1,128)S(1)} %slice.31), channel_id=1, source_target_pairs={{0,4},{4,8},{8,12},{12,16},{16,20},{20,24},{24,28},{1,5},{5,9},{9,... | collective-permute-start | bytes 18440 | tf_op jit(solution)/shard_map/ppermute | solution.py:16
  98.7 1.2 copy-start.2
  136.0 6.0 %slice-start = ((s8[4718592]{0:T(1024)(128)(4,1)}), s8[4194304]{0:T(1024)(128)(4,1)S(1)}, s32[]{:S(2)}) async-start(s8[4718592]{0:T(1024)(128)(4,1)} %bitcast.88), calls=%async_computation.2 | async-start | bytes 8388608
  137.7 4.4 %copy-start.3 = (f32[319,1536]{1,0:T(8,128)S(1)}, f32[319,1536]{1,0:T(8,128)}, u32[]{:S(2)}) copy-start(f32[319,1536]{1,0:T(8,128)} %slice.33) | copy-start | bytes 5879812
  137.7 4.4 %slice-start.1 = ((s8[4718592]{0:T(1024)(128)(4,1)}), s8[524288]{0:T(1024)(128)(4,1)S(1)}, s32[]{:S(2)}) async-start(s8[4718592]{0:T(1024)(128)(4,1)} %bitcast.88), calls=%async_computation.3 | async-start | bytes 1048576
Sparse Core Ops, SparseCore 0:
  9.6 40.1 all-gather.6
  51.4 37.4 all-gather.8
where the time goes:
time: 152 us
  blocking collectives  86.4 us (57%)
  matrix products  24.5 us (16%)
  between operations  15 us (10%)
  waiting for transfers between devices  12.7 us (8%)
  local copies, waits for them, and re-layouts  5.63 us (4%)
  starting transfers between devices  4.76 us (3%)
  other arithmetic  2.75 us (2%)
    all_gather x1, blocking collectives, per_device(): lax.all_gather(back_vector, 'seq', axis=0, tiled=True)  32.6 us
    all_gather x1, blocking collectives, per_device(): lax.all_gather(last_state, 'seq', axis=0, tiled=True)  30.7 us
    unnamed x1, blocking collectives  23.1 us
    all_gather x1, waiting for transfers between devices, per_device(): lax.all_gather(key_weight, 'dp', axis=0, tiled=True)  10.6 us
    dot_general x1, matrix products, per_device(): key_rows = jnp.dot(token_rows, full_key, preferred_element_type=jnp.float32)  4.83 us
    ppermute x2, starting transfers between devices, shifted(): return lax.ppermute(block, axis, route)  4.68 us
    dot_general x1, matrix products, per_device(): lax.dot_general(query_grad, full_query, contract_last, preferred_element_...  4.34 us
    dot_general x1, matrix products, per_device(): jnp.dot(token_rows, full_query, preferred_element_type=jnp.float32)  4.17 us
  transfers between devices with their start and end apart: 4, of which 2 were waited for; matrix products, arithmetic and copies ran while one was open for 9% of the time, Pallas kernels for 0%

commit v1 on v0

--- a/solution.py
+++ b/solution.py
@@ -8,6 +8,27 @@
 exact = lax.Precision.HIGHEST
 contract_last = (((1,), (1,)), ((), ()))
 contract_first = (((0,), (0,)), ((), ()))
+
+
+def laid_out(blocks, dim):
+    dims = list(blocks.shape[1:])
+    dims[dim] *= blocks.shape[0]
+    return jnp.moveaxis(blocks, 0, dim).reshape(dims)
+
+
+def collected_by_bits(array, axis):
+    size, here = (lax.axis_size(axis), lax.axis_index(axis))
+    blocks, bit = (array[None], 1)
+    while bit < size:
+        other = lax.ppermute(blocks, axis, [(i, i ^ bit) for i in range(size)])
+        low = here & bit == 0
+        blocks = jnp.concatenate([jnp.where(low, blocks, other), jnp.where(low, other, blocks)])
+        bit *= 2
+    return blocks
+
+
+def collect(array, axis, dim):
+    return laid_out(collected_by_bits(array, axis), dim)
 
 
 def shifted(block, axis, distance):
@@ -97,7 +118,7 @@
         lax.all_gather(last_log, "seq", axis=0, tiled=True),
         lax.all_gather(last_state, "seq", axis=0, tiled=True),
         lax.all_gather(last_log, "seq", axis=0, tiled=True),
-        lax.all_gather(back_vector, "seq", axis=0, tiled=True),
+        collect(back_vector, "seq", 0),
     )
     state_in = carry_from(summaries[0], summaries[1], shard_index, True)
     grad_in = carry_from(summaries[2], summaries[3], shard_index, False)

time: 152 us -> 133 us (0.88)
  blocking collectives: 86.4 us -> 53.8 us
  starting transfers between devices: 4.76 us -> 12.9 us
  matrix products: 24.5 us -> 26.7 us
  waiting for transfers between devices: 12.7 us -> 14.4 us
    all_gather x1 -> x0, blocking collectives: 32.6 us -> none  [per_device(): lax.all_gather(back_vector, 'seq', axis=0, tiled=True)]
    ppermute x0 -> x3, starting transfers between devices: none -> 7.84 us  [collected_by_bits(): other = lax.ppermute(blocks, axis, [(i, i ^ bit) for i in range(size)])]
    dot_general x1, matrix products: 2.85 us -> 5.13 us  [per_device(): lax.dot_general(key_grad, full_key, contract_last, preferred_element_type...]
    unnamed x25 -> x34, local copies, waits for them, and re-layouts: 2.31 us -> 4.38 us
  transfers between devices with their start and end apart: 4 -> 7, of which waited for: 2 -> 3; matrix products, arithmetic and copies ran while one was open for 9% -> 17% of each run, Pallas kernels for 0% -> 0%
where the time goes in v1:
time: 133 us; the launch traced here: 132 us
  blocking collectives  53.8 us (40%)
  matrix products  26.7 us (20%)
  between operations  15.1 us (11%)
  waiting for transfers between devices  14.4 us (11%)
  starting transfers between devices  12.9 us (10%)
  local copies, waits for them, and re-layouts  6.44 us (5%)
  other arithmetic  2.95 us (2%)
    all_gather x1, blocking collectives, per_device(): lax.all_gather(last_state, 'seq', axis=0, tiled=True)  30.7 us
    unnamed x1, blocking collectives  23.1 us
    all_gather x1, waiting for transfers between devices, per_device(): lax.all_gather(key_weight, 'dp', axis=0, tiled=True)  10.8 us
    ppermute x3, starting transfers between devices, collected_by_bits(): other = lax.ppermute(blocks, axis, [(i, i ^ bit) for i in range(size)])  7.84 us
    dot_general x1, matrix products, per_device(): lax.dot_general(key_grad, full_key, contract_last, preferred_element_type...  5.13 us
    ppermute x2, starting transfers between devices, shifted(): return lax.ppermute(block, axis, route)  4.98 us
    dot_general x1, matrix products, per_device(): lax.dot_general(query_grad, full_query, contract_last, preferred_element_...  4.86 us
    unnamed x34, local copies, waits for them, and re-layouts  4.38 us
  transfers between devices with their start and end apart: 7, of which 3 were waited for; matrix products, arithmetic and copies ran while one was open for 17% of the time, Pallas kernels for 0%

profile of v1, /device:TPU:0, one launch (start us, length us, event | category | flops | bytes accessed | tf_op | source)
XLA Modules:
  0.0 132.2 jit_solution(12041642143235311803)
XLA Ops:
  10.8 1.3 bitcast_dynamic-update-slice_fusion
  12.1 23.1 %all-reduce = f32[8]{0:T(128)S(1)} all-reduce(f32[8]{0:T(128)S(1)} %bitcast_dynamic-update-slice_fusion), channel_id=2, replica_groups=mesh['seq'=8,'dp'=4] {'seq'}, use_global_device_ids=true, to_apply=%add | all-reduce | flops 8 | bytes 64
  36.1 0.9 fusion.24
  37.0 30.7 %all-gather.1 = f32[8,1,1536]{2,1,0:T(1,128)S(1)} all-gather(f32[1,1,1536]{2,1,0:T(1,128)S(1)} %slice_bitcast_fusion), channel_id=1, replica_groups=mesh['seq'=8,'dp'=4] {'seq'}, dimensions={0}, use_global_device_ids=true | all-gather | bytes 55296 | tf_op jit(solution)/shard_map/all_gather | solution.py:119
  69.6 1.5 %fusion.8 = f32[320]{0:T(512)S(1)} fusion(bf16[1,320,1536]{2,1,0:T(8,128)(2,1)S(1)} %copy-done.5, f32[1536]{0:T(1024)S(1)} %convolution_reduce_fusion.2, f32[320]{0:T(512)S(1)} %get-tuple-element.6, f32[128,1536]{1,0:T(8,128)S(1)} %fusion.24, f32[128]{0:T(128)S(1)} %get-tuple-element.17, s32[320]{0:T(512)S(1)} %broadcast_add_fusion), kind=kOutput, calls=%fused_computation.22 | convolution fusion | flops 757866176 | bytes 1779968 | tf_op jit(solution)/shard_map/dot_general | solution.py:126
  71.1 4.2 %multiply_reduce_fusion.4 = (f32[320]{0:T(512)S(1)}, f32[320,1536]{1,0:T(8,128)S(1)}) fusion(bf16[1536,1536]{1,0:T(8,128)(2,1)} %all-gather.5.cloned.1.call-done, bf16[1,320,1536]{2,1,0:T(8,128)(2,1)S(1)} %copy-done), kind=kOutput, calls=%fused_computation.20 | convolution fusion | flops 1510932224 | bytes 7668992 | tf_op jit(solution)/shard_map/dot_general | solution.py:81
  75.5 1.1 copy-done.1
  76.6 1.3 collective-permute-start.1
  78.1 10.8 %all-gather.7.cloned.1.call-done = bf16[1536,1536]{1,0:T(8,128)(2,1)} async-done(((bf16[384,1536]{1,0:T(8,128)(2,1)}), bf16[1536,1536]{1,0:T(8,128)(2,1)}) %all-gather.7.cloned.1.call-update) | async-done | bytes 4718608 | tf_op jit(solution)/shard_map/all_gather | solution.py:78
  88.9 4.2 %multiply_reduce_fusion.1 = (f32[320]{0:T(512)S(1)}, f32[320]{0:T(512)S(1)}, f32[320,1536]{1,0:T(8,128)S(1)}) fusion(f32[1,1536]{1,0:T(1,128)S(1)} %collective-permute-done.1, f32[319,1536]{1,0:T(8,128)S(1)} %slice.33, bf16[1536,1536]{1,0:T(8,128)(2,1)} %all-gather.7.cloned.1.call-done, bf16[1,320,1536]{2,1,0:T(8,128)(2,1)S(1)} %copy-done), kind=kOutput, calls=%fused_computation.16 | convolution fusion | flops 1512406528 | bytes 9636352 | tf_op jit(solution)/shard_map/dot_general | solution.py:80
  93.3 1.0 copy-done.7
  94.3 3.7 %collective-permute-start = (f32[1,1536]{1,0:T(1,128)S(1)}, f32[1,1536]{1,0:T(1,128)S(1)}, u32[]{:S(2)}, u32[]{:S(2)}) collective-permute-start(f32[1,1536]{1,0:T(1,128)S(1)} %slice.31), channel_id=1, source_target_pairs={{0,4},{4,8},{8,12},{12,16},{16,20},{20,24},{24,28},{1,5},{5,9},{9,... | collective-permute-start | bytes 18440 | tf_op jit(solution)/shard_map/ppermute | solution.py:37
  98.1 1.1 collective-permute-done
  99.2 0.9 multiply_reduce_fusion
  100.4 1.2 fusion.7
  101.6 0.9 fusion.9
  103.1 2.4 %collective-permute-start.2 = (f32[1,1,1536]{2,1,0:T(1,128)S(1)}, f32[1,1,1536]{2,1,0:T(1,128)S(1)}, u32[]{:S(2)}, u32[]{:S(2)}) collective-permute-start(f32[1,1,1536]{2,1,0:T(1,128)S(1)} %broadcast_in_dim.69), channel_id=1, source_target_pairs={{0,4},{4,0},{8,12},{12,8},{16,20},{20,16},{24,28},{28,24},{1,5},{5... | collective-permute-start | bytes 18440 | tf_op jit(solution)/shard_map/ppermute | solution.py:23
  106.0 1.0 collective-permute-done.2
  107.1 3.0 %collective-permute-start.3 = (f32[2,1,1536]{2,1,0:T(1,128)S(1)}, f32[2,1,1536]{2,1,0:T(1,128)S(1)}, u32[]{:S(2)}, u32[]{:S(2)}) collective-permute-start(f32[2,1,1536]{2,1,0:T(1,128)S(1)} %pad_maximum_fusion.4), channel_id=1, source_target_pairs={{0,8},{4,12},{8,0},{12,4},{16,24},{20,28},{24,16},{28,20},{1,9},{5... | collective-permute-start | bytes 36872 | tf_op jit(solution)/shard_map/ppermute | solution.py:23
  110.1 4.9 %fusion.10 = f32[320,1536]{1,0:T(8,128)S(1)} fusion(bf16[1536,1536]{1,0:T(8,128)(2,1)} %all-gather.5.cloned.1.call-done, f32[320,1536]{1,0:T(8,128)} %copy-done.1, f32[319,1536]{1,0:T(8,128)S(1)} %bitcast.85, f32[1,1536]{1,0:T(1,128)S(1)} %collective-permute-done, f32[320]{0:T(512)S(1)} %get-tuple-element.22, f32[320]{0:T(512)S(1)} %select_select_fusion, ...), kind=kOutput, calls=%fused_computation.27 | convolution fusion | flops 1512898560 | bytes 10620672 | tf_op jit(solution)/shard_map/dot_general | solution.py:141
  115.0 2.5 %collective-permute-start.4 = (f32[4,1,1536]{2,1,0:T(1,128)S(1)}, f32[4,1,1536]{2,1,0:T(1,128)S(1)}, u32[]{:S(2)}, u32[]{:S(2)}) collective-permute-start(f32[4,1,1536]{2,1,0:T(1,128)S(1)} %pad_maximum_fusion.3), channel_id=1, source_target_pairs={{0,16},{4,20},{8,24},{12,28},{16,0},{20,4},{24,8},{28,12},{1,17},{... | collective-permute-start | bytes 73736 | tf_op jit(solution)/shard_map/ppermute | solution.py:23
  117.5 5.1 %fusion.2 = bf16[1,320,1536]{2,1,0:T(8,128)(2,1)} fusion(f32[320,1536]{1,0:T(8,128)S(1)} %fusion.10, bf16[1536,1536]{1,0:T(8,128)(2,1)} %all-gather.7.cloned.1.call-done, f32[320,1536]{1,0:T(8,128)S(1)} %copy-done.8, f32[1,1536]{1,0:T(1,128)S(1)} %collective-permute-done.1, f32[319,1536]{1,0:T(8,128)S(1)} %copy-done.10, f32[320]{0:T(512)S(1)} %get-tuple-element.14, ...), kind=kOutput, calls=%fused_computation.4 | convolution fusion | flops 1513390080 | bytes 11602432 | tf_op jit(solution)/shard_map/dot_general | solution.py:144
  122.8 0.8 convolution_reduce_fusion.1
  123.6 1.7 %fusion.5 = bf16[1,128,1536]{2,1,0:T(8,128)(2,1)} fusion(f32[128,1536]{1,0:T(8,128)S(1)} %copy-done.4, f32[1536]{0:T(1024)S(1)} %convolution_reduce_fusion.1, f32[128]{0:T(128)S(1)} %get-tuple-element.16, f32[128]{0:T(128)S(1)} %bitcast_select_fusion, f32[128]{0:T(128)S(1)} %reduce), kind=kOutput, calls=%fused_computation.9 | convolution fusion | flops 302841856 | bytes 1187328 | tf_op jit(solution)/shard_map/dot_general | solution.py:131
  (75 shorter events, 7.9 us)
Async XLA Ops:
  7.2 63.9 %copy-start = (bf16[1,320,1536]{2,1,0:T(8,128)(2,1)S(1)}, bf16[1,320,1536]{2,1,0:T(8,128)(2,1)}, u32[]{:S(2)}) copy-start(bf16[1,320,1536]{2,1,0:T(8,128)(2,1)} %param.8) | copy-start | bytes 2949124
  7.2 3.1 %copy-start.14 = (u32[32]{0:T(128)S(1)}, u32[32]{0:T(128)}, u32[]{:S(2)}) copy-start(u32[32]{0:T(128)} %constant.59) | copy-start | bytes 388
  7.2 2.2 %copy-start.13 = (s32[1,128]{1,0:T(1,128)S(1)}, s32[1,128]{1,0:T(1,128)}, u32[]{:S(2)}) copy-start(s32[1,128]{1,0:T(1,128)} %param.13) | copy-start | bytes 1540
  7.2 28.9 %copy-start.11 = (bf16[1,128,1536]{2,1,0:T(8,128)(2,1)S(1)}, bf16[1,128,1536]{2,1,0:T(8,128)(2,1)}, u32[]{:S(2)}) copy-start(bf16[1,128,1536]{2,1,0:T(8,128)(2,1)} %param.10) | copy-start | bytes 1179652
  7.2 61.4 %copy-start.12 = (s32[1,128]{1,0:T(1,128)S(1)}, s32[1,128]{1,0:T(1,128)}, u32[]{:S(2)}) copy-start(s32[1,128]{1,0:T(1,128)} %param.11) | copy-start | bytes 1540
  7.2 62.3 %copy-start.5 = (bf16[1,320,1536]{2,1,0:T(8,128)(2,1)S(1)}, bf16[1,320,1536]{2,1,0:T(8,128)(2,1)}, u32[]{:S(2)}) copy-start(bf16[1,320,1536]{2,1,0:T(8,128)(2,1)} %param.9) | copy-start | bytes 2949124
  7.2 63.8 %all-gather.5.cloned.1.call-start = ((), (), s32[]{:S(2)}) async-start(), calls=%async_computation | async-start | bytes 5898240 | tf_op jit(solution)/shard_map/all_gather | solution.py:77
  8.0 80.9 %all-gather.7.cloned.1.call-start = ((), (), s32[]{:S(2)}) async-start(), calls=%async_computation.1 | async-start | bytes 5898240 | tf_op jit(solution)/shard_map/all_gather | solution.py:78
  75.2 1.4 %copy-start.1 = (f32[320,1536]{1,0:T(8,128)}, f32[320,1536]{1,0:T(8,128)S(1)}, u32[]{:S(2)}) copy-start(f32[320,1536]{1,0:T(8,128)S(1)} %get-tuple-element.19) | copy-start | bytes 5898244
  76.6 12.3 %collective-permute-start.1 = (f32[1,1536]{1,0:T(1,128)S(1)}, f32[1,1536]{1,0:T(1,128)S(1)}, u32[]{:S(2)}, u32[]{:S(2)}) collective-permute-start(f32[1,1536]{1,0:T(1,128)S(1)} %slice.34), channel_id=1, source_target_pairs={{4,0},{8,4},{12,8},{16,12},{20,16},{24,20},{28,24},{5,1},{9,5},{13... | collective-permute-start | bytes 18440 | tf_op jit(solution)/shard_map/ppermute | solution.py:37
  78.1 15.0 %copy-start.9 = (f32[319,1536]{1,0:T(8,128)}, f32[319,1536]{1,0:T(8,128)S(1)}, u32[]{:S(2)}) copy-start(f32[319,1536]{1,0:T(8,128)S(1)} %slice.33) | copy-start | bytes 5879812
  93.1 1.3 copy-start.7
  93.1 6.1 %copy-start.2 = (f32[320,1536]{1,0:T(8,128)S(1)}, f32[320,1536]{1,0:T(8,128)}, u32[]{:S(2)}) copy-start(f32[320,1536]{1,0:T(8,128)} %copy-done.1) | copy-start | bytes 5898244
  94.3 4.9 %collective-permute-start = (f32[1,1536]{1,0:T(1,128)S(1)}, f32[1,1536]{1,0:T(1,128)S(1)}, u32[]{:S(2)}, u32[]{:S(2)}) collective-permute-start(f32[1,1536]{1,0:T(1,128)S(1)} %slice.31), channel_id=1, source_target_pairs={{0,4},{4,8},{8,12},{12,16},{16,20},{20,24},{24,28},{1,5},{5,9},{9,... | collective-permute-start | bytes 18440 | tf_op jit(solution)/shard_map/ppermute | solution.py:37
  99.2 1.2 copy-start.6
  101.6 0.9 copy-start.3
  103.1 4.0 %collective-permute-start.2 = (f32[1,1,1536]{2,1,0:T(1,128)S(1)}, f32[1,1,1536]{2,1,0:T(1,128)S(1)}, u32[]{:S(2)}, u32[]{:S(2)}) collective-permute-start(f32[1,1,1536]{2,1,0:T(1,128)S(1)} %broadcast_in_dim.69), channel_id=1, source_target_pairs={{0,4},{4,0},{8,12},{12,8},{16,20},{20,16},{24,28},{28,24},{1,5},{5... | collective-permute-start | bytes 18440 | tf_op jit(solution)/shard_map/ppermute | solution.py:23
  107.1 7.9 %collective-permute-start.3 = (f32[2,1,1536]{2,1,0:T(1,128)S(1)}, f32[2,1,1536]{2,1,0:T(1,128)S(1)}, u32[]{:S(2)}, u32[]{:S(2)}) collective-permute-start(f32[2,1,1536]{2,1,0:T(1,128)S(1)} %pad_maximum_fusion.4), channel_id=1, source_target_pairs={{0,8},{4,12},{8,0},{12,4},{16,24},{20,28},{24,16},{28,20},{1,9},{5... | collective-permute-start | bytes 36872 | tf_op jit(solution)/shard_map/ppermute | solution.py:23
  110.1 7.5 %copy-start.8 = (f32[320,1536]{1,0:T(8,128)S(1)}, f32[320,1536]{1,0:T(8,128)}, u32[]{:S(2)}) copy-start(f32[320,1536]{1,0:T(8,128)} %copy-done.7) | copy-start | bytes 5898244
  110.1 7.5 %copy-start.10 = (f32[319,1536]{1,0:T(8,128)S(1)}, f32[319,1536]{1,0:T(8,128)}, u32[]{:S(2)}) copy-start(f32[319,1536]{1,0:T(8,128)} %copy-done.9) | copy-start | bytes 5879812
  115.0 7.7 %collective-permute-start.4 = (f32[4,1,1536]{2,1,0:T(1,128)S(1)}, f32[4,1,1536]{2,1,0:T(1,128)S(1)}, u32[]{:S(2)}, u32[]{:S(2)}) collective-permute-start(f32[4,1,1536]{2,1,0:T(1,128)S(1)} %pad_maximum_fusion.3), channel_id=1, source_target_pairs={{0,16},{4,20},{8,24},{12,28},{16,0},{20,4},{24,8},{28,12},{1,17},{... | collective-permute-start | bytes 73736 | tf_op jit(solution)/shard_map/ppermute | solution.py:23
  117.5 6.1 %copy-start.4 = (f32[128,1536]{1,0:T(8,128)S(1)}, f32[128,1536]{1,0:T(8,128)}, u32[]{:S(2)}) copy-start(f32[128,1536]{1,0:T(8,128)} %copy-done.3) | copy-start | bytes 2359300
Sparse Core Ops, SparseCore 0:
  9.6 40.1 all-gather.4
  51.4 37.4 all-gather.6
